TPU v7x, 32 devices: a whole 2x2x4 slice. The times are simulated.
32 devices in a mesh: grp: 8 (over y, x, core), ent: 4 (over z).
Axes of the slice: x: 2, y: 2, z: 4, core: 2. Of those that a mesh axis runs over, the one named last changes fastest.
Arguments:
- factor: bfloat16 [4096, 256], P(('grp', 'ent')), may hold values from -1.5 to 1.5
- cores: bfloat16 [16, 256, 256], replicated, may hold values from -0.375 to 0.375
- adjacency: int32 [768, 128, 128], P(('grp', 'ent')), may hold values 0 or 1
- tile_rels: int32 [32, 24], P(('grp', 'ent')), may hold values from 0 to 15
- tile_count: int32 [32], P(('grp', 'ent')), may hold values from 1 to 24, 480 in all
- send_lists: int32 [32, 4, 6], P(('grp', 'ent')), may hold values from 0 to 7
Outputs:
- factor_grad: float32 [4096, 256], P(('grp', 'ent'))
All inputs are finite; a program needn't handle non-finite values. No bound on the sum of `adjacency` or of `tile_count` on one device may be relied on, other than what follows from the above.
Results may differ from a plain program's by a relative error of at most 0.002.
Values may be sent and summed in bfloat16 or wider, within the bound.
No kernel may reach another device: no remote copies, remote signals or barrier semaphores. Data moves between devices by JAX's collectives and lax.ppermute only.
A program may use at most 64 MiB of HBM per device.

v0:
```python
import jax
import jax.numpy as jnp
from jax import lax
from jax.sharding import PartitionSpec as P

LOSS_SCALE = 0.0625


def on_device(factor, cores, adjacency, tile_rels, tile_count, send_lists):
    ent_count = lax.axis_size("ent")
    grp_count = lax.axis_size("grp")
    my_ent = lax.axis_index("ent")
    tiles = tile_rels.shape[1]
    block = factor.shape[0]
    width = factor.shape[1]
    per_relay = tiles // ent_count
    slots = ent_count * per_relay
    relations = tile_rels[0]
    routes = send_lists[0].reshape(slots)
    group_blocks = lax.all_gather(factor[None], "grp", axis=0, tiled=True)
    outgoing = group_blocks[routes].reshape(ent_count, per_relay, block, width)
    arrived = lax.all_to_all(outgoing, "ent", split_axis=0, concat_axis=0, tiled=True).reshape(
        slots, block, width
    )
    tile_ids = jnp.arange(tiles, dtype=jnp.int32)
    slot_of_tile = (my_ent + tile_ids) % ent_count * per_relay + tile_ids // ent_count
    factor_panels = arrived[slot_of_tile]
    live = (tile_ids < tile_count[0]).astype(jnp.float32)
    by_relation = jnp.einsum(
        "br,krs->kbs", factor, cores, preferred_element_type=jnp.float32
    ).astype(jnp.bfloat16)
    mapped_tiles = by_relation[relations]
    predicted_scores = jnp.einsum(
        "ogj,omj->ogm", mapped_tiles, factor_panels, preferred_element_type=jnp.float32
    )
    score_residual = (
        (predicted_scores - adjacency.astype(jnp.float32)) * (LOSS_SCALE * live)[:, None, None]
    ).astype(jnp.bfloat16)
    relation_product = jnp.einsum(
        "xmw,xwe->xme", score_residual, factor_panels, preferred_element_type=jnp.float32
    ).astype(jnp.bfloat16)
    row_grad = jnp.einsum(
        "tbs,trs->br", relation_product, cores[relations], preferred_element_type=jnp.float32
    )
    slot_ids = jnp.arange(slots, dtype=jnp.int32)
    tile_of_slot = slot_ids % per_relay * ent_count + (slot_ids // per_relay - my_ent) % ent_count
    column_terms = jnp.einsum(
        "yzj,yzh->yjh", score_residual, mapped_tiles, preferred_element_type=jnp.float32
    ).astype(jnp.bfloat16)
    sent_terms = column_terms[tile_of_slot].reshape(ent_count, per_relay, block, width)
    returned = (
        lax.all_to_all(sent_terms, "ent", split_axis=0, concat_axis=0, tiled=True)
        .reshape(slots, block * width)
        .astype(jnp.float32)
    )
    owner_onehot = (routes[:, None] == jnp.arange(grp_count, dtype=jnp.int32)[None, :]).astype(
        jnp.float32
    )
    owner_terms = jnp.dot(
        owner_onehot.T,
        returned,
        precision=lax.Precision.HIGHEST,
        preferred_element_type=jnp.float32,
    )
    owner_part = lax.psum_scatter(
        owner_terms.reshape(grp_count, block, width), "grp", scatter_dimension=0, tiled=True
    )
    return row_grad + owner_part[0]


def solution(mesh):
    in_specs = (
        P(("grp", "ent"), None),
        P(),
        P(("grp", "ent"), None, None),
        P(("grp", "ent"), None),
        P(("grp", "ent")),
        P(("grp", "ent"), None, None),
    )
    out_specs = P(("grp", "ent"), None)
    return jax.shard_map(
        on_device, mesh=mesh, in_specs=in_specs, out_specs=out_specs, check_vma=False
    )
```

profile of v0, /device:TPU:0, one launch (start us, length us, event | category | flops | bytes accessed | tf_op | source)
XLA Modules:
  0.0 166.0 jit_solution(857811333616795226)
XLA Ops:
  6.5 0.0 copy-start
  6.5 0.9 reshape_squeeze.3
  7.5 11.6 %all-gather = bf16[1024,256]{1,0:T(8,128)(2,1)S(1)} all-gather(bf16[128,256]{1,0:T(8,128)(2,1)} %param.6), channel_id=2, replica_groups=mesh['grp'=8,'ent'=4] {'grp'}, dimensions={0}, use_global_device_ids=true | all-gather | bytes 589824 | tf_op jit(solution)/shard_map/all_gather | solution.py:20
  19.1 1.9 %gather_fusion.1 = bf16[24,128,256]{2,1,0:T(8,128)(2,1)} fusion(bf16[8,128,256]{2,1,0:T(8,128)(2,1)S(1)} %bitcast.50, s32[1024]{0:T(1024)S(1)} %pad_clamp_fusion.2), kind=kCustom, calls=%fused_computation.1 | custom fusion | bytes 3145824 | tf_op jit(solution)/shard_map/gather | solution.py:21
  20.9 5.0 %all-to-all-start = ((bf16[4,6,128,256]{3,2,1,0:T(8,128)(2,1)}), bf16[4,6,128,256]{3,2,1,0:T(8,128)(2,1)}, u32[]{:S(2)}, u32[]{:S(2)}) async-start(bf16[4,6,128,256]{3,2,1,0:T(8,128)(2,1)} %bitcast.51), calls=%async_computation | async-start | bytes 3145728 | tf_op jit(solution)/shard_map/all_to_all | solution.py:22
  26.6 0.0 copy-done.4
  26.6 0.0 copy-done
  26.6 0.8 fusion.4
  27.4 1.9 %gather_fusion = bf16[24,128,256]{1,2,0:T(8,128)(2,1)} fusion(bf16[16,128,256]{1,2,0:T(8,128)(2,1)S(1)} %fusion.4, s32[1024]{0:T(1024)S(1)} %pad_clamp_fusion.3), kind=kCustom, calls=%fused_computation | custom fusion | bytes 3145824 | tf_op jit(solution)/shard_map/gather | solution.py:32
  29.4 34.1 %all-to-all-done = bf16[4,6,128,256]{3,2,1,0:T(8,128)(2,1)} async-done(((bf16[4,6,128,256]{3,2,1,0:T(8,128)(2,1)}), bf16[4,6,128,256]{3,2,1,0:T(8,128)(2,1)}, u32[]{:S(2)}, u32[]{:S(2)}) %all-to-all-start) | async-done | bytes 1572896 | tf_op jit(solution)/shard_map/all_to_all | solution.py:22
  63.5 3.3 %gather_fusion.2 = bf16[24,128,256]{2,1,0:T(8,128)(2,1)} fusion(bf16[24,128,256]{2,1,0:T(8,128)(2,1)} %bitcast.7, s32[1024]{0:T(1024)S(1)} %pad_clamp_fusion.1), kind=kCustom, calls=%fused_computation.2 | custom fusion | bytes 3145824 | tf_op jit(solution)/shard_map/gather | solution.py:27
  66.8 3.2 %multiply_convert_fusion = bf16[24,128,128]{2,1,0:T(8,128)(2,1)S(1)} fusion(s32[24,128,128]{2,1,0:T(8,128)} %param.8, bf16[24,128,256]{1,2,0:T(8,128)(2,1)} %gather_fusion, bf16[24,128,256]{2,1,0:T(8,128)(2,1)} %gather_fusion.2, f32[24]{0:T(128)S(1)} %compare_select_fusion.8), kind=kOutput, calls=%fused_computation.10 | convolution fusion | flops 202899456 | bytes 5505120 | tf_op jit(solution)/shard_map/ogj,omj->ogm/dot_general | solution.py:33
  70.0 1.8 %convolution_convert_fusion = bf16[24,128,256]{2,1,0:T(8,128)(2,1)} fusion(bf16[24,128,128]{2,1,0:T(8,128)(2,1)S(1)} %multiply_convert_fusion, bf16[24,128,256]{1,2,0:T(8,128)(2,1)S(1)} %copy-done.1), kind=kOutput, calls=%fused_computation.5 | convolution fusion | flops 202113024 | bytes 3932160 | tf_op jit(solution)/shard_map/yzj,yzh->yjh/dot_general | solution.py:47
  71.7 3.2 %gather_fusion.4 = bf16[24,128,256]{2,1,0:T(8,128)(2,1)} fusion(bf16[24,128,256]{2,1,0:T(8,128)(2,1)} %convolution_convert_fusion, s32[1024]{0:T(1024)S(1)} %pad_clamp_fusion), kind=kCustom, calls=%fused_computation.4 | custom fusion | bytes 3145824 | tf_op jit(solution)/shard_map/gather | solution.py:50
  75.0 4.5 %all-to-all-start.1 = ((bf16[4,6,128,256]{3,2,1,0:T(8,128)(2,1)}), bf16[4,6,128,256]{3,2,1,0:T(8,128)(2,1)}, u32[]{:S(2)}, u32[]{:S(2)}) async-start(bf16[4,6,128,256]{3,2,1,0:T(8,128)(2,1)} %bitcast.52), calls=%async_computation.1 | async-start | bytes 3145728 | tf_op jit(solution)/shard_map/all_to_all | solution.py:52
  79.5 0.0 reduce-scatter.2.cloned.1.call-start
  79.5 0.1 eq.19
  79.6 36.6 %all-to-all-done.1 = bf16[4,6,128,256]{3,2,1,0:T(8,128)(2,1)} async-done(((bf16[4,6,128,256]{3,2,1,0:T(8,128)(2,1)}), bf16[4,6,128,256]{3,2,1,0:T(8,128)(2,1)}, u32[]{:S(2)}, u32[]{:S(2)}) %all-to-all-start.1) | async-done | bytes 1572896 | tf_op jit(solution)/shard_map/all_to_all | solution.py:52
  116.2 2.6 %fusion = f32[8,128,256]{2,0,1:T(8,128)S(1)} fusion(s32[24]{0:T(128)S(1)} %eq.19, bf16[3,8,128,256]{3,2,1,0:T(8,128)(2,1)} %bitcast.19), kind=kOutput, calls=%fused_computation.7 | convolution fusion | flops 12583104 | bytes 2621536 | tf_op jit(solution)/shard_map/dot_general | solution.py:59
  118.8 1.3 copy.17
  120.2 0.0 reduce-scatter.2.cloned.1.call-update
  120.2 2.5 %gather_fusion.3 = bf16[24,256,256]{2,1,0:T(8,128)(2,1)} fusion(bf16[16,256,256]{2,1,0:T(8,128)(2,1)S(1)} %copy-done, s32[1024]{0:T(1024)S(1)} %pad_clamp_fusion.3), kind=kCustom, calls=%fused_computation.3 | custom fusion | bytes 6291552 | tf_op jit(solution)/shard_map/gather | solution.py:43
  122.7 31.8 %reduce-scatter.2.cloned.1.call-done = f32[1,128,256]{2,1,0:T(8,128)} async-done(((f32[8,128,256]{2,1,0:T(8,128)}), f32[1,128,256]{2,1,0:T(8,128)}) %reduce-scatter.2.cloned.1.call-update) | async-done | bytes 131088 | tf_op jit(solution)/shard_map/reduce_scatter | solution.py:65
  154.5 4.6 %fusion.6 = f32[128,256]{1,0:T(8,128)} fusion(bf16[24,256,256]{2,1,0:T(8,128)(2,1)} %gather_fusion.3, bf16[24,128,128]{2,1,0:T(8,128)(2,1)S(1)} %multiply_convert_fusion, bf16[24,128,256]{2,1,0:T(8,128)(2,1)} %gather_fusion.2, f32[1,128,256]{2,1,0:T(8,128)} %reduce-scatter.2.cloned.1.call-done), kind=kOutput, calls=%fused_computation.15 | convolution fusion | flops 604798976 | bytes 5767168 | tf_op jit(solution)/shard_map/tbs,trs->br/dot_general | solution.py:42
  (16 shorter events, 0.1 us)
Async XLA Ops:
  6.5 20.1 %copy-start = (bf16[16,256,256]{2,1,0:T(8,128)(2,1)S(1)}, bf16[16,256,256]{2,1,0:T(8,128)(2,1)}, u32[]{:S(2)}) copy-start(bf16[16,256,256]{2,1,0:T(8,128)(2,1)} %param.7) | copy-start | bytes 6291460
  20.9 5.7 %copy-start.4 = (s32[1,24]{1,0:T(1,128)S(1)}, s32[1,24]{1,0:T(1,128)}, u32[]{:S(2)}) copy-start(s32[1,24]{1,0:T(1,128)} %param.9) | copy-start | bytes 292
  20.9 5.7 %copy-start.2 = (bf16[128,256]{1,0:T(8,128)(2,1)S(1)}, bf16[128,256]{1,0:T(8,128)(2,1)}, u32[]{:S(2)}) copy-start(bf16[128,256]{1,0:T(8,128)(2,1)} %param.6) | copy-start | bytes 196612
  20.9 42.6 %all-to-all-start = ((bf16[4,6,128,256]{3,2,1,0:T(8,128)(2,1)}), bf16[4,6,128,256]{3,2,1,0:T(8,128)(2,1)}, u32[]{:S(2)}, u32[]{:S(2)}) async-start(bf16[4,6,128,256]{3,2,1,0:T(8,128)(2,1)} %bitcast.51), calls=%async_computation | async-start | bytes 3145728 | tf_op jit(solution)/shard_map/all_to_all | solution.py:22
  66.8 3.2 %copy-start.1 = (bf16[24,128,256]{1,2,0:T(8,128)(2,1)S(1)}, bf16[24,128,256]{1,2,0:T(8,128)(2,1)}, u32[]{:S(2)}) copy-start(bf16[24,128,256]{1,2,0:T(8,128)(2,1)} %gather_fusion) | copy-start | bytes 4718596
  75.0 4.5 %copy-start.3 = (s32[1,4,6]{2,1,0:T(4,128)S(1)}, s32[1,4,6]{2,1,0:T(4,128)}, u32[]{:S(2)}) copy-start(s32[1,4,6]{2,1,0:T(4,128)} %param.11) | copy-start | bytes 292
  75.0 41.2 %all-to-all-start.1 = ((bf16[4,6,128,256]{3,2,1,0:T(8,128)(2,1)}), bf16[4,6,128,256]{3,2,1,0:T(8,128)(2,1)}, u32[]{:S(2)}, u32[]{:S(2)}) async-start(bf16[4,6,128,256]{3,2,1,0:T(8,128)(2,1)} %bitcast.52), calls=%async_computation.1 | async-start | bytes 3145728 | tf_op jit(solution)/shard_map/all_to_all | solution.py:52
  79.5 75.0 %reduce-scatter.2.cloned.1.call-start = ((), (), s32[]{:S(2)}) async-start(), calls=%async_computation.3 | async-start | bytes 1179648 | tf_op jit(solution)/shard_map/reduce_scatter | solution.py:65
Sparse Core Ops, SparseCore 0:
  120.3 34.1 reduce-scatter.1
where the time goes:
time: 166 us
  waiting for transfers between devices  103 us (62%)
  local copies, waits for them, and re-layouts  15.2 us (9%)
  between operations  14.2 us (9%)
  matrix products  12.9 us (8%)
  blocking collectives  11.6 us (7%)
  starting transfers between devices  9.52 us (6%)
    all_to_all x1, waiting for transfers between devices, on_device(): lax.all_to_all(sent_terms, 'ent', split_axis=0, concat_axis=0, tiled=True)  36.6 us
    all_to_all x1, waiting for transfers between devices, on_device(): lax.all_to_all(outgoing, 'ent', split_axis=0, concat_axis=0, tiled=True)  34.1 us
    reduce_scatter x1, waiting for transfers between devices, on_device(): lax.psum_scatter(owner_terms.reshape(grp_count, block, width), 'grp', sca...  31.8 us
    all_gather x1, blocking collectives, on_device(): group_blocks = lax.all_gather(factor[None], 'grp', axis=0, tiled=True)  11.6 us
    all_to_all x1, starting transfers between devices, on_device(): lax.all_to_all(outgoing, 'ent', split_axis=0, concat_axis=0, tiled=True)  5 us
    dot_general x1, matrix products, on_device(): jnp.einsum('tbs,trs->br', relation_product, cores[relations], preferred_e...  4.58 us
    all_to_all x1, starting transfers between devices, on_device(): lax.all_to_all(sent_terms, 'ent', split_axis=0, concat_axis=0, tiled=True)  4.48 us
  transfers between devices with their start and end apart: 3, of which 3 were waited for; matrix products, arithmetic and copies ran while one was open for 3% of the time, Pallas kernels for 0%

commit v1 on v0

--- a/solution.py
+++ b/solution.py
@@ -17,7 +17,14 @@
     slots = ent_count * per_relay
     relations = tile_rels[0]
     routes = send_lists[0].reshape(slots)
-    group_blocks = lax.all_gather(factor[None], "grp", axis=0, tiled=True)
+    ways, here, turn = (lax.axis_size("grp"), lax.axis_index("grp"), factor[None].shape[0])
+    line, have = (factor[None], 1)
+    while have < ways:
+        line = jnp.concatenate(
+            [line, lax.ppermute(line, "grp", [(d, (d - have) % ways) for d in range(ways)])], axis=0
+        )
+        have = 2 * have
+    group_blocks = jnp.roll(line, here * turn, axis=0)
     outgoing = group_blocks[routes].reshape(ent_count, per_relay, block, width)
     arrived = lax.all_to_all(outgoing, "ent", split_axis=0, concat_axis=0, tiled=True).reshape(
         slots, block, width

time: 166 us -> 180 us (1.084)
  blocking collectives: 11.6 us -> 0 us
  waiting for transfers between devices: 103 us -> 113 us
  local copies, waits for them, and re-layouts: 15.2 us -> 22.2 us
  starting transfers between devices: 9.52 us -> 14.6 us
    all_gather x1 -> x0, blocking collectives: 11.6 us -> none  [on_device(): group_blocks = lax.all_gather(factor[None], 'grp', axis=0, tiled=True)]
    ppermute x0 -> x3, waiting for transfers between devices: none -> 10.3 us  [on_device(): lax.ppermute(line, 'grp', [(d, (d - have) % ways) for d in range(ways)])]
    unnamed x10 -> x17, local copies, waits for them, and re-layouts: 0.02 us -> 5.42 us
    ppermute x0 -> x3, starting transfers between devices: none -> 5.11 us  [on_device(): lax.ppermute(line, 'grp', [(d, (d - have) % ways) for d in range(ways)])]
    reduce_scatter x1, waiting for transfers between devices: 31.8 us -> 34.5 us  [on_device(): lax.psum_scatter(owner_terms.reshape(grp_count, block, width), 'grp', sca...]
    all_to_all x1, waiting for transfers between devices: 34.1 us -> 32.3 us  [on_device(): lax.all_to_all(outgoing, 'ent', split_axis=0, concat_axis=0, tiled=True)]
  transfers between devices with their start and end apart: 3 -> 6, of which waited for: 3 -> 5; matrix products, arithmetic and copies ran while one was open for 3% -> 5% of each run, Pallas kernels for 0% -> 0%
where the time goes in v1:
time: 180 us; the launch traced here: 179 us
  waiting for transfers between devices  113 us (63%)
  local copies, waits for them, and re-layouts  22.2 us (12%)
  starting transfers between devices  14.6 us (8%)
  between operations  14.2 us (8%)
  matrix products  12.9 us (7%)
    all_to_all x1, waiting for transfers between devices, on_device(): lax.all_to_all(sent_terms, 'ent', split_axis=0, concat_axis=0, tiled=True)  36.4 us
    reduce_scatter x1, waiting for transfers between devices, on_device(): lax.psum_scatter(owner_terms.reshape(grp_count, block, width), 'grp', sca...  34.5 us
    all_to_all x1, waiting for transfers between devices, on_device(): lax.all_to_all(outgoing, 'ent', split_axis=0, concat_axis=0, tiled=True)  32.3 us
    ppermute x3, waiting for transfers between devices, on_device(): lax.ppermute(line, 'grp', [(d, (d - have) % ways) for d in range(ways)])  10.3 us
    unnamed x17, local copies, waits for them, and re-layouts  5.42 us
    ppermute x3, starting transfers between devices, on_device(): lax.ppermute(line, 'grp', [(d, (d - have) % ways) for d in range(ways)])  5.11 us
    all_to_all x1, starting transfers between devices, on_device(): lax.all_to_all(outgoing, 'ent', split_axis=0, concat_axis=0, tiled=True)  5 us
    dot_general x1, matrix products, on_device(): jnp.einsum('tbs,trs->br', relation_product, cores[relations], preferred_e...  4.59 us
  transfers between devices with their start and end apart: 6, of which 5 were waited for; matrix products, arithmetic and copies ran while one was open for 5% of the time, Pallas kernels for 0%

profile of v1, /device:TPU:0, one launch (start us, length us, event | category | flops | bytes accessed | tf_op | source)
XLA Modules:
  0.0 179.1 jit_solution(15211434512584239237)
XLA Ops:
  6.5 3.3 %collective-permute-start = (bf16[1,128,256]{2,1,0:T(8,128)(2,1)}, bf16[1,128,256]{2,1,0:T(8,128)(2,1)S(1)}, u32[]{:S(2)}, u32[]{:S(2)}) collective-permute-start(bf16[1,128,256]{2,1,0:T(8,128)(2,1)} %bitcast.54), channel_id=1, source_target_pairs={{0,28},{4,0},{8,4},{12,8},{16,12},{20,16},{24,20},{28,24},{1,29},{... | collective-permute-start | bytes 196616 | tf_op jit(solution)/shard_map/ppermute | solution.py:24
  9.9 1.5 constant_dynamic-update-slice_fusion.7
  11.4 0.8 reshape_squeeze.3
  12.1 0.9 pad_maximum_fusion.1
  13.7 4.9 %collective-permute-done.1 = bf16[2,128,256]{2,1,0:T(8,128)(2,1)S(1)} collective-permute-done((bf16[2,128,256]{2,1,0:T(8,128)(2,1)S(1)}, bf16[2,128,256]{2,1,0:T(8,128)(2,1)S(1)}, u32[]{:S(2)}, u32[]{:S(2)}) %collective-permute-start.1) | collective-permute-done | bytes 131104 | tf_op jit(solution)/shard_map/ppermute | solution.py:24
  18.7 0.9 pad_maximum_fusion
  19.6 1.0 collective-permute-start.2
  21.9 5.4 %collective-permute-done.2 = bf16[4,128,256]{2,1,0:T(8,128)(2,1)S(1)} collective-permute-done((bf16[4,128,256]{2,1,0:T(8,128)(2,1)S(1)}, bf16[4,128,256]{2,1,0:T(8,128)(2,1)S(1)}, u32[]{:S(2)}, u32[]{:S(2)}) %collective-permute-start.2) | collective-permute-done | bytes 262176 | tf_op jit(solution)/shard_map/ppermute | solution.py:24
  30.6 1.1 constant_dynamic-slice_fusion
  31.7 1.9 %gather_fusion.1 = bf16[24,128,256]{2,1,0:T(8,128)(2,1)} fusion(bf16[8,128,256]{2,1,0:T(8,128)(2,1)S(1)} %constant_dynamic-slice_fusion, s32[1024]{0:T(1024)S(1)} %pad_clamp_fusion.2), kind=kCustom, calls=%fused_computation.1 | custom fusion | bytes 3145824 | tf_op jit(solution)/shard_map/gather | solution.py:28
  33.5 5.0 %all-to-all-start = ((bf16[4,6,128,256]{3,2,1,0:T(8,128)(2,1)}), bf16[4,6,128,256]{3,2,1,0:T(8,128)(2,1)}, u32[]{:S(2)}, u32[]{:S(2)}) async-start(bf16[4,6,128,256]{3,2,1,0:T(8,128)(2,1)} %bitcast.52), calls=%async_computation | async-start | bytes 3145728 | tf_op jit(solution)/shard_map/all_to_all | solution.py:29
  40.0 1.9 %gather_fusion = bf16[24,128,256]{1,2,0:T(8,128)(2,1)} fusion(bf16[16,128,256]{1,2,0:T(8,128)(2,1)S(1)} %fusion.4, s32[1024]{0:T(1024)S(1)} %get-tuple-element.6), kind=kCustom, calls=%fused_computation | custom fusion | bytes 3145824 | tf_op jit(solution)/shard_map/gather | solution.py:39
  42.0 32.3 %all-to-all-done = bf16[4,6,128,256]{3,2,1,0:T(8,128)(2,1)} async-done(((bf16[4,6,128,256]{3,2,1,0:T(8,128)(2,1)}), bf16[4,6,128,256]{3,2,1,0:T(8,128)(2,1)}, u32[]{:S(2)}, u32[]{:S(2)}) %all-to-all-start) | async-done | bytes 1572896 | tf_op jit(solution)/shard_map/all_to_all | solution.py:29
  74.3 3.3 %gather_fusion.2 = bf16[24,128,256]{2,1,0:T(8,128)(2,1)} fusion(bf16[24,128,256]{2,1,0:T(8,128)(2,1)} %bitcast.7, s32[1024]{0:T(1024)S(1)} %get-tuple-element.5), kind=kCustom, calls=%fused_computation.2 | custom fusion | bytes 3145824 | tf_op jit(solution)/shard_map/gather | solution.py:34
  77.5 3.2 %multiply_convert_fusion = bf16[24,128,128]{2,1,0:T(8,128)(2,1)S(1)} fusion(s32[24,128,128]{2,1,0:T(8,128)} %param.8, bf16[24,128,256]{1,2,0:T(8,128)(2,1)} %gather_fusion, bf16[24,128,256]{2,1,0:T(8,128)(2,1)} %gather_fusion.2, f32[24]{0:T(128)S(1)} %compare_select_fusion.8), kind=kOutput, calls=%fused_computation.10 | convolution fusion | flops 202899456 | bytes 5505120 | tf_op jit(solution)/shard_map/ogj,omj->ogm/dot_general | solution.py:40
  80.7 1.8 convolution_convert_fusion
  82.5 3.3 %gather_fusion.4 = bf16[24,128,256]{2,1,0:T(8,128)(2,1)} fusion(bf16[24,128,256]{2,1,0:T(8,128)(2,1)} %convolution_convert_fusion, s32[1024]{0:T(1024)S(1)} %pad_clamp_fusion), kind=kCustom, calls=%fused_computation.4 | custom fusion | bytes 3145824 | tf_op jit(solution)/shard_map/gather | solution.py:57
  85.8 4.5 %all-to-all-start.1 = ((bf16[4,6,128,256]{3,2,1,0:T(8,128)(2,1)}), bf16[4,6,128,256]{3,2,1,0:T(8,128)(2,1)}, u32[]{:S(2)}, u32[]{:S(2)}) async-start(bf16[4,6,128,256]{3,2,1,0:T(8,128)(2,1)} %bitcast.53), calls=%async_computation.1 | async-start | bytes 3145728 | tf_op jit(solution)/shard_map/all_to_all | solution.py:59
  90.4 36.4 %all-to-all-done.1 = bf16[4,6,128,256]{3,2,1,0:T(8,128)(2,1)} async-done(((bf16[4,6,128,256]{3,2,1,0:T(8,128)(2,1)}), bf16[4,6,128,256]{3,2,1,0:T(8,128)(2,1)}, u32[]{:S(2)}, u32[]{:S(2)}) %all-to-all-start.1) | async-done | bytes 1572896 | tf_op jit(solution)/shard_map/all_to_all | solution.py:59
  126.7 2.6 %fusion = f32[8,128,256]{2,0,1:T(8,128)S(1)} fusion(s32[24]{0:T(128)S(1)} %eq.22, bf16[3,8,128,256]{3,2,1,0:T(8,128)(2,1)} %bitcast.19), kind=kOutput, calls=%fused_computation.7 | convolution fusion | flops 12583104 | bytes 2621536 | tf_op jit(solution)/shard_map/dot_general | solution.py:66
  129.4 1.3 copy.17
  130.7 2.5 %gather_fusion.3 = bf16[24,256,256]{2,1,0:T(8,128)(2,1)} fusion(bf16[16,256,256]{2,1,0:T(8,128)(2,1)S(1)} %copy-done, s32[1024]{0:T(1024)S(1)} %get-tuple-element.6), kind=kCustom, calls=%fused_computation.3 | custom fusion | bytes 6291552 | tf_op jit(solution)/shard_map/gather | solution.py:50
  133.2 34.5 %reduce-scatter.2.cloned.1.call-done = f32[1,128,256]{2,1,0:T(8,128)} async-done(((f32[8,128,256]{2,1,0:T(8,128)}), f32[1,128,256]{2,1,0:T(8,128)}) %reduce-scatter.2.cloned.1.call-update) | async-done | bytes 131088 | tf_op jit(solution)/shard_map/reduce_scatter | solution.py:72
  167.7 4.6 %fusion.6 = f32[128,256]{1,0:T(8,128)} fusion(bf16[24,256,256]{2,1,0:T(8,128)(2,1)} %gather_fusion.3, bf16[24,128,128]{2,1,0:T(8,128)(2,1)S(1)} %multiply_convert_fusion, bf16[24,128,256]{2,1,0:T(8,128)(2,1)} %gather_fusion.2, f32[1,128,256]{2,1,0:T(8,128)} %reduce-scatter.2.cloned.1.call-done), kind=kOutput, calls=%fused_computation.15 | convolution fusion | flops 604798976 | bytes 5767168 | tf_op jit(solution)/shard_map/tbs,trs->br/dot_general | solution.py:49
  (31 shorter events, 6.4 us)
Async XLA Ops:
  6.5 32.7 %copy-start = (bf16[16,256,256]{2,1,0:T(8,128)(2,1)S(1)}, bf16[16,256,256]{2,1,0:T(8,128)(2,1)}, u32[]{:S(2)}) copy-start(bf16[16,256,256]{2,1,0:T(8,128)(2,1)} %param.7) | copy-start | bytes 6291460
  6.5 21.4 %copy-start.2 = (bf16[128,256]{1,0:T(8,128)(2,1)S(1)}, bf16[128,256]{1,0:T(8,128)(2,1)}, u32[]{:S(2)}) copy-start(bf16[128,256]{1,0:T(8,128)(2,1)} %param.6) | copy-start | bytes 196612
  6.5 5.6 %collective-permute-start = (bf16[1,128,256]{2,1,0:T(8,128)(2,1)}, bf16[1,128,256]{2,1,0:T(8,128)(2,1)S(1)}, u32[]{:S(2)}, u32[]{:S(2)}) collective-permute-start(bf16[1,128,256]{2,1,0:T(8,128)(2,1)} %bitcast.54), channel_id=1, source_target_pairs={{0,28},{4,0},{8,4},{12,8},{16,12},{20,16},{24,20},{28,24},{1,29},{... | collective-permute-start | bytes 196616 | tf_op jit(solution)/shard_map/ppermute | solution.py:24
  13.0 5.7 %collective-permute-start.1 = (bf16[2,128,256]{2,1,0:T(8,128)(2,1)S(1)}, bf16[2,128,256]{2,1,0:T(8,128)(2,1)S(1)}, u32[]{:S(2)}, u32[]{:S(2)}) collective-permute-start(bf16[2,128,256]{2,1,0:T(8,128)(2,1)S(1)} %pad_maximum_fusion.1), channel_id=1, source_target_pairs={{0,24},{4,28},{8,0},{12,4},{16,8},{20,12},{24,16},{28,20},{1,25},{... | collective-permute-start | bytes 393224 | tf_op jit(solution)/shard_map/ppermute | solution.py:24
  19.6 7.7 %collective-permute-start.2 = (bf16[4,128,256]{2,1,0:T(8,128)(2,1)S(1)}, bf16[4,128,256]{2,1,0:T(8,128)(2,1)S(1)}, u32[]{:S(2)}, u32[]{:S(2)}) collective-permute-start(bf16[4,128,256]{2,1,0:T(8,128)(2,1)S(1)} %pad_maximum_fusion), channel_id=1, source_target_pairs={{0,16},{4,20},{8,24},{12,28},{16,0},{20,4},{24,8},{28,12},{1,17},{... | collective-permute-start | bytes 786440 | tf_op jit(solution)/shard_map/ppermute | solution.py:24
  33.5 5.7 %copy-start.4 = (s32[1,24]{1,0:T(1,128)S(1)}, s32[1,24]{1,0:T(1,128)}, u32[]{:S(2)}) copy-start(s32[1,24]{1,0:T(1,128)} %param.9) | copy-start | bytes 292
  33.5 40.7 %all-to-all-start = ((bf16[4,6,128,256]{3,2,1,0:T(8,128)(2,1)}), bf16[4,6,128,256]{3,2,1,0:T(8,128)(2,1)}, u32[]{:S(2)}, u32[]{:S(2)}) async-start(bf16[4,6,128,256]{3,2,1,0:T(8,128)(2,1)} %bitcast.52), calls=%async_computation | async-start | bytes 3145728 | tf_op jit(solution)/shard_map/all_to_all | solution.py:29
  77.5 3.2 %copy-start.1 = (bf16[24,128,256]{1,2,0:T(8,128)(2,1)S(1)}, bf16[24,128,256]{1,2,0:T(8,128)(2,1)}, u32[]{:S(2)}) copy-start(bf16[24,128,256]{1,2,0:T(8,128)(2,1)} %gather_fusion) | copy-start | bytes 4718596
  85.8 4.5 %copy-start.3 = (s32[1,4,6]{2,1,0:T(4,128)S(1)}, s32[1,4,6]{2,1,0:T(4,128)}, u32[]{:S(2)}) copy-start(s32[1,4,6]{2,1,0:T(4,128)} %param.11) | copy-start | bytes 292
  85.8 41.0 %all-to-all-start.1 = ((bf16[4,6,128,256]{3,2,1,0:T(8,128)(2,1)}), bf16[4,6,128,256]{3,2,1,0:T(8,128)(2,1)}, u32[]{:S(2)}, u32[]{:S(2)}) async-start(bf16[4,6,128,256]{3,2,1,0:T(8,128)(2,1)} %bitcast.53), calls=%async_computation.1 | async-start | bytes 3145728 | tf_op jit(solution)/shard_map/all_to_all | solution.py:59
  90.2 77.4 %reduce-scatter.2.cloned.1.call-start = ((), (), s32[]{:S(2)}) async-start(), calls=%async_computation.3 | async-start | bytes 1179648 | tf_op jit(solution)/shard_map/reduce_scatter | solution.py:72
Sparse Core Ops, SparseCore 0:
  130.9 36.7 reduce-scatter.1
